TPU v7x, 256 devices: a whole 4x4x8 slice. The times are simulated.
256 devices in a mesh: blk: 64 (over z, x_lo, y), circ: 4 (over x_hi, core).
Axes of the slice: x: 4 (x_hi: 2, x_lo: 2; x = x_hi * 2 + x_lo), y: 4, z: 8, core: 2. Of those that a mesh axis runs over, the one named last changes fastest.
Arguments:
- panels: float32 [4, 8192], P(None, ('blk', 'circ')), may hold values from -2 to 2, as said below
- node_of_panel: int32 [8192], P(('blk', 'circ')), may hold values from 0 to 2047, as said below
- stiffener_rows: int32 [32], replicated, may hold values from 0 to 511
- density_start: float32 [16, 8192], P(None, ('blk', 'circ')), may hold values from -6 to 6
- motion_start: float32 [16, 512, 1024], P(None, 'blk', 'circ'), may hold values from -6 to 6
- force: float32 [16, 512, 1024], P(None, 'blk', 'circ'), may hold values from -128 to 128
- stiffness: float32 [512, 1024], P('blk', 'circ'), may hold values from 0.5 to 2
Outputs:
- source_density: float32 [16, 8192], P(None, ('blk', 'circ'))
- surface_pressure: float32 [16, 8192], P(None, ('blk', 'circ'))
- shell_motion: float32 [16, 512, 1024], P(None, 'blk', 'circ')
Inputs may be any that keep to these rules, and one draw needn't show every extreme that they name: `panels`: every panel lies between 0.98 and 1.02 from the z axis, with z between -2 and 2 and area between 0.5 and 2 times 8 pi / 8192. `node_of_panel`: counted as row * 256 + column within the tile of the device that holds the panel. `stiffener_rows`: A row may be listed more than once.
All inputs are finite; a program needn't handle non-finite values.
Results may differ from a plain program's by a relative error of at most 0.0029.
Values may be sent and summed in bfloat16 or wider, within the bound.
No kernel may reach another device: no remote copies, remote signals or barrier semaphores. Data moves between devices by JAX's collectives and lax.ppermute only.
A program may use at most 64 MiB of HBM per device.

v0:
```python
import math

import jax
import jax.numpy as jnp
from jax import lax
from jax.sharding import PartitionSpec as P

ITERS = 4
SWEEPS = 2


wave_number = 4.0
single_scale = 30.0
double_scale = 6.0
hoop_spring = 40.0
inertia_term = 4.0
loss_factor = 0.2
relaxation = 0.3


def padded(block, sides, width):
    for axis, dim in sides:
        count = lax.axis_size(axis)
        forward = [(i, i + 1) for i in range(count - 1)]
        forward.append((count - 1, 0))
        backward = [(target, source) for source, target in forward]
        low = lax.ppermute(
            lax.slice_in_dim(block, block.shape[dim] - width, None, axis=dim), axis, forward
        )
        high = lax.ppermute(lax.slice_in_dim(block, 0, width, axis=dim), axis, backward)
        block = jnp.concatenate([low, block, high], axis=dim)
    return block


def kernel_blocks(targets, sources):
    radial = jnp.sqrt(targets[0] * targets[0] + targets[1] * targets[1])
    normal_x = (targets[0] / radial)[:, None]
    normal_y = (targets[1] / radial)[:, None]
    delta_x = targets[0][:, None] - sources[0][None, :]
    delta_y = targets[1][:, None] - sources[1][None, :]
    delta_z = targets[2][:, None] - sources[2][None, :]
    areas = sources[3][None, :]
    dist_sq = delta_x * delta_x + delta_y * delta_y + delta_z * delta_z + areas / math.pi
    distance = jnp.sqrt(dist_sq)
    inverse = 1.0 / distance
    phase_arg = wave_number * distance
    cosine = jnp.cos(phase_arg)
    sine_part = jnp.sin(phase_arg)
    weight = areas * (1.0 / (4.0 * math.pi)) * inverse
    single = single_scale * weight
    double = double_scale * weight * (normal_x * delta_x + normal_y * delta_y) * inverse * inverse
    real_stack = jnp.concatenate(
        [single * cosine, double * (-cosine - phase_arg * sine_part)], axis=0
    )
    imag_stack = jnp.concatenate(
        [single * sine_part, double * (phase_arg * cosine - sine_part)], axis=0
    )
    return (real_stack.astype(jnp.bfloat16), imag_stack.astype(jnp.bfloat16))


def form_kernels(targets, sources):
    width = sources.shape[1]
    block_cols = math.gcd(width, 1024)
    block_count = width // block_cols
    source_blocks = jnp.transpose(sources.reshape(4, block_count, block_cols), (1, 0, 2))
    real_blocks, imag_blocks = lax.map(lambda block: kernel_blocks(targets, block), source_blocks)
    rows_out = real_blocks.shape[1]
    real_stack = jnp.transpose(real_blocks, (1, 0, 2)).reshape(rows_out, width)
    imag_stack = jnp.transpose(imag_blocks, (1, 0, 2)).reshape(rows_out, width)
    return (real_stack, imag_stack)


def fold_columns(real_stack, imag_stack):

    def fold_step(running, shard_piece, first_col):
        half = shard_piece.shape[0] // 2
        rotated = jnp.concatenate([-shard_piece[half:], shard_piece[:half]], axis=0)
        first = jnp.einsum("lc,rc->lr", shard_piece, real_stack, preferred_element_type=jnp.float32)
        second = jnp.einsum("lc,rc->lr", rotated, imag_stack, preferred_element_type=jnp.float32)
        return first + second

    return fold_step


def laplace_inner(extended):
    return (
        extended[..., 2:, 1:-1]
        + extended[..., :-2, 1:-1]
        + extended[..., 1:-1, 2:]
        + extended[..., 1:-1, :-2]
        - 4.0 * extended[..., 1:-1, 1:-1]
    )


def clear_outside(extended, width, blk_index, axial):
    total_rows = axial * lax.axis_size("blk")
    rows_here = blk_index * axial - width + jnp.arange(axial + 2 * width, dtype=jnp.int32)
    inside = (rows_here >= 0) & (rows_here < total_rows)
    return jnp.where(inside[:, None], extended, 0.0)


def relax(motion, bend, load, stiffness, hoop_rows):
    half = motion.shape[0] // 2
    shift = hoop_spring * hoop_rows - inertia_term
    applied_re = bend[:half] - loss_factor * bend[half:] + shift * motion[:half]
    applied_im = bend[half:] + loss_factor * bend[:half] + shift * motion[half:]
    resid_re = load[:half] - applied_re
    resid_im = load[half:] - applied_im
    diag_re = 20.0 * stiffness + shift
    diag_im = 20.0 * loss_factor * stiffness
    denom = diag_re * diag_re + diag_im * diag_im
    update_re = (resid_re * diag_re + resid_im * diag_im) / denom
    update_im = (resid_im * diag_re - resid_re * diag_im) / denom
    return motion + relaxation * jnp.concatenate([update_re, update_im], axis=0)


def per_device(
    panels, node_of_panel, stiffener_rows, density_start, motion_start, force, stiffness
):
    panel_dev = panels.shape[1]
    channels = density_start.shape[0]
    axial, circum = stiffness.shape
    blk_index = lax.axis_index("blk")
    devices = lax.axis_size("blk") * lax.axis_size("circ")
    rows_global = blk_index * axial + jnp.arange(axial, dtype=jnp.int32)
    hoop_rows = jnp.any(rows_global[:, None] == stiffener_rows[None, :], axis=1).astype(
        jnp.float32
    )[:, None]
    panel_weight = panels[3] * (panel_dev * devices / (8.0 * math.pi))
    sources = lax.all_gather(panels, ("blk", "circ"), axis=1, tiled=True)
    target_rows = panels.shape[1]
    real_stack, imag_stack = form_kernels(panels, sources)
    fold_step = fold_columns(real_stack, imag_stack)
    density = density_start
    motion = motion_start
    pressure = jnp.zeros_like(density_start)
    for round_index in range(ITERS):
        flat_motion = motion.reshape(channels, axial * circum)
        neumann = jnp.take(flat_motion, node_of_panel, axis=1)
        density_bf = density.astype(jnp.bfloat16)
        start_sum = jnp.zeros((channels, 2 * target_rows), jnp.float32)
        combined = fold_step(
            start_sum, lax.all_gather(density_bf, ("blk", "circ"), axis=1, tiled=True), jnp.int32(0)
        )
        single_part = combined[:, :target_rows]
        double_part = combined[:, target_rows:]
        pressure = single_part
        density = 0.5 * density + neumann - double_part
        fluid = jnp.zeros((channels, axial * circum), jnp.float32)
        fluid = fluid.at[:, node_of_panel].add(panel_weight[None, :] * pressure)
        load = force - fluid.reshape(channels, axial, circum)
        for sweep_index in range(SWEEPS):
            motion_ext = padded(motion, (("blk", 1), ("circ", 2)), 1)
            motion_ext = clear_outside(motion_ext, 1, blk_index, axial)
            moment = stiffness * laplace_inner(motion_ext)
            moment_ext = padded(moment, (("blk", 1), ("circ", 2)), 1)
            moment_ext = clear_outside(moment_ext, 1, blk_index, axial)
            bend = laplace_inner(moment_ext)
            motion = relax(motion, bend, load, stiffness, hoop_rows)
    return (density, pressure, motion)


def solution(mesh):
    in_specs = (
        P(None, ("blk", "circ")),
        P(("blk", "circ")),
        P(),
        P(None, ("blk", "circ")),
        P(None, "blk", "circ"),
        P(None, "blk", "circ"),
        P("blk", "circ"),
    )
    out_specs = (P(None, ("blk", "circ")), P(None, ("blk", "circ")), P(None, "blk", "circ"))
    return jax.shard_map(
        per_device, mesh=mesh, in_specs=in_specs, out_specs=out_specs, check_vma=False
    )
```

profile of v0, /device:TPU:128, one launch (start us, length us, event | category | flops | bytes accessed | tf_op | source)
XLA Modules:
  0.0 2006.9 jit_solution(11817012427763911444)
XLA Ops:
  1.6 3.6 collective-permute-start.1
  7.2 347.0 %all-gather = f32[256,32,4]{1,2,0:T(4,128)S(1)} all-gather(f32[1,32,4]{1,2,0:T(4,128)S(1)} %bitcast.201), channel_id=1, replica_groups=mesh['blk'=64,'circ'=4] {'blk','circ'}, dimensions={0}, use_global_device_ids=true | all-gather | bytes 131584 | tf_op jit(solution)/shard_map/all_gather | solution.py:130
  354.7 11.7 while.15
  368.7 341.9 %all-gather.1 = bf16[256,32,16]{1,2,0:T(8,128)(2,1)S(1)} all-gather(bf16[1,32,16]{1,2,0:T(8,128)(2,1)S(1)} %convert_bitcast_fusion.3), channel_id=1, replica_groups=mesh['blk'=64,'circ'=4] {'blk','circ'}, dimensions={0}, use_global_device_ids=true | all-gather | bytes 263168 | tf_op jit(solution)/shard_map/all_gather | solution.py:143
  716.6 344.9 %all-gather.2 = bf16[256,32,16]{1,2,0:T(8,128)(2,1)S(1)} all-gather(bf16[1,32,16]{1,2,0:T(8,128)(2,1)S(1)} %get-tuple-element.276), channel_id=1, replica_groups=mesh['blk'=64,'circ'=4] {'blk','circ'}, dimensions={0}, use_global_device_ids=true | all-gather | bytes 263168 | tf_op jit(solution)/shard_map/all_gather | solution.py:143
  1072.3 4.7 collective-permute-done.2
  1081.4 4.3 collective-permute-done.4
  1088.5 3.9 collective-permute-done.6
  1096.9 4.9 collective-permute-done.8
  1104.5 4.0 collective-permute-done.10
  1112.9 4.3 collective-permute-done.12
  1128.0 4.3 collective-permute-done.16
  1135.0 4.1 collective-permute-done.18
  1144.3 4.0 collective-permute-done.20
  1158.3 346.9 %all-gather.3 = bf16[256,32,16]{1,2,0:T(8,128)(2,1)S(1)} all-gather(bf16[1,32,16]{1,2,0:T(8,128)(2,1)S(1)} %get-tuple-element.171), channel_id=1, replica_groups=mesh['blk'=64,'circ'=4] {'blk','circ'}, dimensions={0}, use_global_device_ids=true | all-gather | bytes 263168 | tf_op jit(solution)/shard_map/all_gather | solution.py:143
  1510.2 4.4 collective-permute-done.26
  1519.0 4.3 collective-permute-done.28
  1526.0 4.2 collective-permute-done.30
  1533.5 343.6 %all-gather.4 = bf16[256,32,16]{1,2,0:T(8,128)(2,1)S(1)} all-gather(bf16[1,32,16]{1,2,0:T(8,128)(2,1)S(1)} %get-tuple-element.274), channel_id=1, replica_groups=mesh['blk'=64,'circ'=4] {'blk','circ'}, dimensions={0}, use_global_device_ids=true | all-gather | bytes 263168 | tf_op jit(solution)/shard_map/all_gather | solution.py:143
  1884.1 4.3 collective-permute-done.32
  1907.6 4.2 collective-permute-done.38
  1916.3 5.5 collective-permute-done.40
  1924.5 4.4 collective-permute-done.42
  1933.3 4.3 collective-permute-done.44
  1948.3 4.4 collective-permute-done.48
  1955.5 4.1 collective-permute-done.50
  1963.9 4.3 collective-permute-done.52
  1971.0 3.7 collective-permute-done.54
  1979.2 4.3 collective-permute-done.56
  1986.3 3.9 collective-permute-done.58
  1994.6 4.3 collective-permute-done.60
  2001.7 3.7 collective-permute-done.62
  (355 shorter events, 169.7 us)
Async XLA Ops:
  1.6 1067.7 %collective-permute-start.1 = (f32[16,1,256]{2,1,0:T(1,128)S(1)}, f32[16,1,256]{2,1,0:T(1,128)S(1)}, u32[]{:S(2)}, u32[]{:S(2)}) collective-permute-start(f32[16,1,256]{2,1,0:T(1,128)S(1)} %get-tuple-element.272), channel_id=1, source_target_pairs={{4,0},{8,4},{12,8},{16,12},{20,16},{24,20},{28,24},{32,28},{36,32}... | collective-permute-start | bytes 49160 | tf_op jit(solution)/shard_map/ppermute | solution.py:30
  5.2 1064.1 %collective-permute-start = (f32[16,1,256]{2,1,0:T(1,128)S(1)}, f32[16,1,256]{2,1,0:T(1,128)S(1)}, u32[]{:S(2)}, u32[]{:S(2)}) collective-permute-start(f32[16,1,256]{2,1,0:T(1,128)S(1)} %get-tuple-element.271), channel_id=1, source_target_pairs={{0,4},{4,8},{8,12},{12,16},{16,20},{20,24},{24,28},{28,32},{32,36}... | collective-permute-start | bytes 49160 | tf_op jit(solution)/shard_map/ppermute | solution.py:27
  1069.8 7.2 collective-permute-start.2
  1077.7 8.0 collective-permute-start.4
  1086.0 6.4 collective-permute-start.6
  1093.4 8.4 collective-permute-start.8
  1102.0 6.5 collective-permute-start.10
  1109.2 8.0 collective-permute-start.12
  1117.4 6.0 collective-permute-start.14
  1124.2 8.0 collective-permute-start.16
  1132.5 6.7 collective-permute-start.18
  1140.3 8.0 collective-permute-start.20
  1148.7 6.1 collective-permute-start.22
  1156.2 351.2 %collective-permute-start.25 = (f32[16,1,256]{2,1,0:T(1,128)S(1)}, f32[16,1,256]{2,1,0:T(1,128)S(1)}, u32[]{:S(2)}, u32[]{:S(2)}) collective-permute-start(f32[16,1,256]{2,1,0:T(1,128)S(1)} %get-tuple-element.258), channel_id=1, source_target_pairs={{4,0},{8,4},{12,8},{16,12},{20,16},{24,20},{28,24},{32,28},{36,32}... | collective-permute-start | bytes 49160 | tf_op jit(solution)/shard_map/ppermute | solution.py:30
  1156.5 350.9 %collective-permute-start.24 = (f32[16,1,256]{2,1,0:T(1,128)S(1)}, f32[16,1,256]{2,1,0:T(1,128)S(1)}, u32[]{:S(2)}, u32[]{:S(2)}) collective-permute-start(f32[16,1,256]{2,1,0:T(1,128)S(1)} %get-tuple-element.257), channel_id=1, source_target_pairs={{0,4},{4,8},{8,12},{12,16},{16,20},{20,24},{24,28},{28,32},{32,36}... | collective-permute-start | bytes 49160 | tf_op jit(solution)/shard_map/ppermute | solution.py:27
  1507.6 6.9 collective-permute-start.26
  1515.2 8.0 collective-permute-start.28
  1523.5 6.8 collective-permute-start.30
  1880.4 8.0 collective-permute-start.32
  1896.6 8.0 collective-permute-start.36
  1905.0 6.7 collective-permute-start.38
  1913.8 8.0 collective-permute-start.40
  1922.0 6.9 collective-permute-start.42
  1929.6 8.0 collective-permute-start.44
  1944.8 8.0 collective-permute-start.48
  1953.0 6.6 collective-permute-start.50
  1960.2 8.0 collective-permute-start.52
  1968.5 6.2 collective-permute-start.54
  1975.5 8.0 collective-permute-start.56
  1983.8 6.4 collective-permute-start.58
  1990.9 8.0 collective-permute-start.60
  1999.2 6.2 collective-permute-start.62
  (51 other events, 3038.8 us)
where the time goes:
time: 2020 us; the launch traced here: 2010 us
  blocking collectives  1720 us (85%)
  waiting for transfers between devices  173 us (9%)
  starting transfers between devices  46.5 us (2%)
  other arithmetic  31.7 us (2%)
  local copies, waits for them, and re-layouts  25.2 us (1%)
    all_gather x4, blocking collectives, per_device(): lax.all_gather(density_bf, ('blk', 'circ'), axis=1, tiled=True)  1380 us
    all_gather x1, blocking collectives, per_device(): sources = lax.all_gather(panels, ('blk', 'circ'), axis=1, tiled=True)  347 us
    ppermute x32, waiting for transfers between devices, padded(): lax.ppermute(lax.slice_in_dim(block, block.shape[dim] - width, None, axis...  122 us
    ppermute x32, waiting for transfers between devices, padded(): lax.ppermute(lax.slice_in_dim(block, 0, width, axis=dim), axis, backward)  50.6 us
  transfers between devices with their start and end apart: 64, of which 59 were waited for; matrix products, arithmetic and copies ran while one was open for 2% of the time, Pallas kernels for 0%

commit v1 on v0

--- a/solution.py
+++ b/solution.py
@@ -18,18 +18,34 @@
 relaxation = 0.3
 
 
-def padded(block, sides, width):
-    for axis, dim in sides:
-        count = lax.axis_size(axis)
-        forward = [(i, i + 1) for i in range(count - 1)]
-        forward.append((count - 1, 0))
-        backward = [(target, source) for source, target in forward]
-        low = lax.ppermute(
-            lax.slice_in_dim(block, block.shape[dim] - width, None, axis=dim), axis, forward
-        )
-        high = lax.ppermute(lax.slice_in_dim(block, 0, width, axis=dim), axis, backward)
-        block = jnp.concatenate([low, block, high], axis=dim)
-    return block
+def gather_columns(block):
+    count = lax.axis_size("blk") * lax.axis_size("circ")
+    index = lax.axis_index("blk") * lax.axis_size("circ") + lax.axis_index("circ")
+    held = block[None]
+    bit = 1
+    while bit < count:
+        pairs = [(i, i ^ bit) for i in range(count)]
+        other = lax.ppermute(held, ("blk", "circ"), pairs)
+        low = (index & bit) == 0
+        first = jnp.where(low, held, other)
+        second = jnp.where(low, other, held)
+        held = jnp.concatenate([first, second], axis=0)
+        bit *= 2
+    return jnp.transpose(held, (1, 0, 2)).reshape(block.shape[0], count * block.shape[1])
+
+
+def laplace_halo(field):
+    rows = lax.axis_size("blk")
+    cols = lax.axis_size("circ")
+    above = lax.ppermute(field[:, -1:, :], "blk", [(i, i + 1) for i in range(rows - 1)])
+    below = lax.ppermute(field[:, :1, :], "blk", [(i + 1, i) for i in range(rows - 1)])
+    left = lax.ppermute(field[:, :, -1:], "circ", [(i, (i + 1) % cols) for i in range(cols)])
+    right = lax.ppermute(field[:, :, :1], "circ", [(i, (i - 1) % cols) for i in range(cols)])
+    down = jnp.concatenate([field[:, 1:, :], below], axis=1)
+    up = jnp.concatenate([above, field[:, :-1, :]], axis=1)
+    east = jnp.concatenate([field[:, :, 1:], right], axis=2)
+    west = jnp.concatenate([left, field[:, :, :-1]], axis=2)
+    return down + up + east + west - 4.0 * field
 
 
 def kernel_blocks(targets, sources):
@@ -82,23 +98,6 @@
     return fold_step
 
 
-def laplace_inner(extended):
-    return (
-        extended[..., 2:, 1:-1]
-        + extended[..., :-2, 1:-1]
-        + extended[..., 1:-1, 2:]
-        + extended[..., 1:-1, :-2]
-        - 4.0 * extended[..., 1:-1, 1:-1]
-    )
-
-
-def clear_outside(extended, width, blk_index, axial):
-    total_rows = axial * lax.axis_size("blk")
-    rows_here = blk_index * axial - width + jnp.arange(axial + 2 * width, dtype=jnp.int32)
-    inside = (rows_here >= 0) & (rows_here < total_rows)
-    return jnp.where(inside[:, None], extended, 0.0)
-
-
 def relax(motion, bend, load, stiffness, hoop_rows):
     half = motion.shape[0] // 2
     shift = hoop_spring * hoop_rows - inertia_term
@@ -127,7 +126,7 @@
         jnp.float32
     )[:, None]
     panel_weight = panels[3] * (panel_dev * devices / (8.0 * math.pi))
-    sources = lax.all_gather(panels, ("blk", "circ"), axis=1, tiled=True)
+    sources = gather_columns(panels)
     target_rows = panels.shape[1]
     real_stack, imag_stack = form_kernels(panels, sources)
     fold_step = fold_columns(real_stack, imag_stack)
@@ -140,7 +139,7 @@
         density_bf = density.astype(jnp.bfloat16)
         start_sum = jnp.zeros((channels, 2 * target_rows), jnp.float32)
         combined = fold_step(
-            start_sum, lax.all_gather(density_bf, ("blk", "circ"), axis=1, tiled=True), jnp.int32(0)
+            start_sum, gather_columns(density_bf), jnp.int32(0)
         )
         single_part = combined[:, :target_rows]
         double_part = combined[:, target_rows:]
@@ -150,12 +149,8 @@
         fluid = fluid.at[:, node_of_panel].add(panel_weight[None, :] * pressure)
         load = force - fluid.reshape(channels, axial, circum)
         for sweep_index in range(SWEEPS):
-            motion_ext = padded(motion, (("blk", 1), ("circ", 2)), 1)
-            motion_ext = clear_outside(motion_ext, 1, blk_index, axial)
-            moment = stiffness * laplace_inner(motion_ext)
-            moment_ext = padded(moment, (("blk", 1), ("circ", 2)), 1)
-            moment_ext = clear_outside(moment_ext, 1, blk_index, axial)
-            bend = laplace_inner(moment_ext)
+            moment = stiffness * laplace_halo(motion)
+            bend = laplace_halo(moment)
             motion = relax(motion, bend, load, stiffness, hoop_rows)
     return (density, pressure, motion)
 

time: 2020 us -> 492 us (0.24)
  blocking collectives: 1720 us -> 0 us
  starting transfers between devices: 46.5 us -> 186 us
  waiting for transfers between devices: 173 us -> 202 us
  local copies, waits for them, and re-layouts: 25.2 us -> 47.9 us
    all_gather x5 -> x0, blocking collectives: 1720 us -> none  [the longest x4 1380 us: per_device(): lax.all_gather(density_bf, ('blk', 'circ'), axis=1, tiled=True)]
    ppermute x64 -> x104, starting transfers between devices: 46.5 us -> 186 us  [the longest x16 57.2 us: laplace_halo(): lax.ppermute(field[:, :1, :], 'blk', [(i + 1, i) for i in range(rows - 1)])]
    ppermute x64 -> x104, waiting for transfers between devices: 173 us -> 202 us  [the longest x40 123 us: gather_columns(): other = lax.ppermute(held, ('blk', 'circ'), pairs)]
  transfers between devices with their start and end apart: 64 -> 104, of which waited for: 59 -> 46; matrix products, arithmetic and copies ran while one was open for 2% -> 9% of each run, Pallas kernels for 0% -> 0%
where the time goes in v1:
time: 492 us; the launch traced here: 484 us
  waiting for transfers between devices  202 us (41%)
  starting transfers between devices  186 us (38%)
  local copies, waits for them, and re-layouts  47.9 us (10%)
  other arithmetic  38.9 us (8%)
  matrix products  5.96 us (1%)
    ppermute x40, waiting for transfers between devices, gather_columns(): other = lax.ppermute(held, ('blk', 'circ'), pairs)  123 us
    ppermute x16, waiting for transfers between devices, laplace_halo(): lax.ppermute(field[:, -1:, :], 'blk', [(i, i + 1) for i in range(rows - 1)])  79 us
    ppermute x16, starting transfers between devices, laplace_halo(): lax.ppermute(field[:, :1, :], 'blk', [(i + 1, i) for i in range(rows - 1)])  57.2 us
    ppermute x16, starting transfers between devices, laplace_halo(): lax.ppermute(field[:, -1:, :], 'blk', [(i, i + 1) for i in range(rows - 1)])  50.7 us
    ppermute x40, starting transfers between devices, gather_columns(): other = lax.ppermute(held, ('blk', 'circ'), pairs)  48.9 us
    ppermute x16, starting transfers between devices, laplace_halo(): lax.ppermute(field[:, :, :1], 'circ', [(i, (i - 1) % cols) for i in range...  26.1 us
  transfers between devices with their start and end apart: 104, of which 46 were waited for; matrix products, arithmetic and copies ran while one was open for 9% of the time, Pallas kernels for 0%

profile of v1, /device:TPU:128, one launch (start us, length us, event | category | flops | bytes accessed | tf_op | source)
XLA Modules:
  0.0 484.2 jit_solution(3485611525478412273)
XLA Ops:
  6.8 4.6 collective-permute-start.16
  37.5 4.0 collective-permute-start.11
  63.5 5.0 %collective-permute-done.5 = bf16[32,16,32]{2,1,0:T(8,128)(2,1)S(1)} collective-permute-done((bf16[32,16,32]{2,1,0:T(8,128)(2,1)S(1)}, bf16[32,16,32]{2,1,0:T(8,128)(2,1)S(1)}, u32[]{:S(2)}, u32[]{:S(2)}) %collective-permute-start.5) | collective-permute-done | bytes 32800 | tf_op jit(solution)/shard_map/ppermute | solution.py:28
  70.3 5.4 %collective-permute-done.14 = f32[64,4,32]{2,1,0:T(4,128)S(1)} collective-permute-done((f32[64,4,32]{2,1,0:T(4,128)S(1)}, f32[64,4,32]{2,1,0:T(4,128)S(1)}, u32[]{:S(2)}, u32[]{:S(2)}) %collective-permute-start.14) | collective-permute-done | bytes 32800 | tf_op jit(solution)/shard_map/ppermute | solution.py:28
  77.2 11.0 %collective-permute-done.6 = bf16[64,16,32]{2,1,0:T(8,128)(2,1)S(1)} collective-permute-done((bf16[64,16,32]{2,1,0:T(8,128)(2,1)S(1)}, bf16[64,16,32]{2,1,0:T(8,128)(2,1)S(1)}, u32[]{:S(2)}, u32[]{:S(2)}) %collective-permute-start.6) | collective-permute-done | bytes 65568 | tf_op jit(solution)/shard_map/ppermute | solution.py:28
  88.9 7.4 %collective-permute-done.15 = f32[128,4,32]{0,2,1:T(8,128)S(1)} collective-permute-done((f32[128,4,32]{0,2,1:T(8,128)S(1)}, f32[128,4,32]{0,2,1:T(8,128)S(1)}, u32[]{:S(2)}, u32[]{:S(2)}) %collective-permute-start.15) | collective-permute-done | bytes 65568 | tf_op jit(solution)/shard_map/ppermute | solution.py:28
  97.9 6.6 %while.15 = (s32[]{:T(128)}, bf16[8,64,1024]{2,1,0:T(8,128)(2,1)S(1)}, bf16[8,64,1024]{2,1,0:T(8,128)(2,1)S(1)}, f32[8,4,1024]{2,0,1:T(8,128)S(1)}, f32[4,32]{1,...) while((s32[]{:T(128)}, ...), condition=%wide.region_1.3_spmd, body=%wide.region_0.2_spmd.sunk | while | flops 1607685 | bytes 845361 | solution.py:82
  133.0 5.4 %collective-permute-done.37 = bf16[32,16,32]{2,1,0:T(8,128)(2,1)S(1)} collective-permute-done((bf16[32,16,32]{2,1,0:T(8,128)(2,1)S(1)}, bf16[32,16,32]{2,1,0:T(8,128)(2,1)S(1)}, u32[]{:S(2)}, u32[]{:S(2)}) %collective-permute-start.37) | collective-permute-done | bytes 32800 | tf_op jit(solution)/shard_map/ppermute | solution.py:28
  139.7 9.3 %collective-permute-start.20 = (f32[16,1,256]{2,1,0:T(1,128)}, f32[16,1,256]{2,1,0:T(1,128)}, u32[]{:S(2)}, u32[]{:S(2)}) collective-permute-start(f32[16,1,256]{2,1,0:T(1,128)} %get-tuple-element.356), channel_id=1, source_target_pairs={{4,0},{8,4},{12,8},{16,12},{20,16},{24,20},{28,24},{32,28},{36,32}... | collective-permute-start | bytes 49160 | tf_op jit(solution)/shard_map/ppermute | solution.py:41
  151.8 11.6 %collective-permute-start.39 = (bf16[128,16,32]{0,2,1:T(8,128)(2,1)S(1)}, bf16[128,16,32]{0,2,1:T(8,128)(2,1)}, u32[]{:S(2)}, u32[]{:S(2)}) collective-permute-start(bf16[128,16,32]{0,2,1:T(8,128)(2,1)S(1)} %pad_maximum_fusion.8), channel_id=1, source_target_pairs={{0,128},{1,129},{2,130},{3,131},{4,132},{5,133},{6,134},{7,135},{8... | collective-permute-start | bytes 393224 | tf_op jit(solution)/shard_map/ppermute | solution.py:28
  186.6 9.3 %collective-permute-start.24 = (f32[16,1,256]{2,1,0:T(1,128)S(1)}, f32[16,1,256]{2,1,0:T(1,128)S(1)}, u32[]{:S(2)}, u32[]{:S(2)}) collective-permute-start(f32[16,1,256]{2,1,0:T(1,128)S(1)} %get-tuple-element.348), channel_id=1, source_target_pairs={{4,0},{8,4},{12,8},{16,12},{20,16},{24,20},{28,24},{32,28},{36,32}... | collective-permute-start | bytes 49160 | tf_op jit(solution)/shard_map/ppermute | solution.py:41
  197.9 7.9 %collective-permute-done.25 = f32[16,1,256]{2,1,0:T(1,128)S(1)} collective-permute-done((f32[16,1,256]{2,1,0:T(1,128)S(1)}, f32[16,1,256]{2,1,0:T(1,128)S(1)}, u32[]{:S(2)}, u32[]{:S(2)}) %collective-permute-start.25) | collective-permute-done | bytes 16416 | tf_op jit(solution)/shard_map/ppermute | solution.py:40
  214.1 5.9 %collective-permute-done.29 = f32[16,1,256]{2,1,0:T(1,128)S(1)} collective-permute-done((f32[16,1,256]{2,1,0:T(1,128)S(1)}, f32[16,1,256]{2,1,0:T(1,128)S(1)}, u32[]{:S(2)}, u32[]{:S(2)}) %collective-permute-start.29) | collective-permute-done | bytes 16416 | tf_op jit(solution)/shard_map/ppermute | solution.py:40
  250.1 3.9 collective-permute-start.45
  254.3 5.7 %collective-permute-done.45 = f32[16,1,256]{2,1,0:T(1,128)S(1)} collective-permute-done((f32[16,1,256]{2,1,0:T(1,128)S(1)}, f32[16,1,256]{2,1,0:T(1,128)S(1)}, u32[]{:S(2)}, u32[]{:S(2)}) %collective-permute-start.45) | collective-permute-done | bytes 16416 | tf_op jit(solution)/shard_map/ppermute | solution.py:40
  268.6 5.9 %collective-permute-done.49 = f32[16,1,256]{2,1,0:T(1,128)S(1)} collective-permute-done((f32[16,1,256]{2,1,0:T(1,128)S(1)}, f32[16,1,256]{2,1,0:T(1,128)S(1)}, u32[]{:S(2)}, u32[]{:S(2)}) %collective-permute-start.49) | collective-permute-done | bytes 16416 | tf_op jit(solution)/shard_map/ppermute | solution.py:40
  283.7 5.0 %collective-permute-done.53 = f32[16,1,256]{2,1,0:T(1,128)S(1)} collective-permute-done((f32[16,1,256]{2,1,0:T(1,128)S(1)}, f32[16,1,256]{2,1,0:T(1,128)S(1)}, u32[]{:S(2)}, u32[]{:S(2)}) %collective-permute-start.53) | collective-permute-done | bytes 16416 | tf_op jit(solution)/shard_map/ppermute | solution.py:40
  290.9 7.8 %collective-permute-done.62 = bf16[64,16,32]{2,1,0:T(8,128)(2,1)} collective-permute-done((bf16[64,16,32]{2,1,0:T(8,128)(2,1)}, bf16[64,16,32]{2,1,0:T(8,128)(2,1)}, u32[]{:S(2)}, u32[]{:S(2)}) %collective-permute-start.62) | collective-permute-done | bytes 65568 | tf_op jit(solution)/shard_map/ppermute | solution.py:28
  301.7 8.7 %collective-permute-done.63 = bf16[128,16,32]{0,2,1:T(8,128)(2,1)S(1)} collective-permute-done((bf16[128,16,32]{0,2,1:T(8,128)(2,1)S(1)}, bf16[128,16,32]{0,2,1:T(8,128)(2,1)S(1)}, u32[]{:S(2)}, u32[]{:S(2)}) %collective-permute-start.63) | collective-permute-done | bytes 131104 | tf_op jit(solution)/shard_map/ppermute | solution.py:28
  324.7 5.6 %collective-permute-start.64 = (f32[16,1,256]{2,1,0:T(1,128)S(1)}, f32[16,1,256]{2,1,0:T(1,128)S(1)}, u32[]{:S(2)}, u32[]{:S(2)}) collective-permute-start(f32[16,1,256]{2,1,0:T(1,128)S(1)} %get-tuple-element.294), channel_id=1, source_target_pairs={{4,0},{8,4},{12,8},{16,12},{20,16},{24,20},{28,24},{32,28},{36,32}... | collective-permute-start | bytes 49160 | tf_op jit(solution)/shard_map/ppermute | solution.py:41
  332.4 7.7 %collective-permute-done.65 = f32[16,1,256]{2,1,0:T(1,128)S(1)} collective-permute-done((f32[16,1,256]{2,1,0:T(1,128)S(1)}, f32[16,1,256]{2,1,0:T(1,128)S(1)}, u32[]{:S(2)}, u32[]{:S(2)}) %collective-permute-start.65) | collective-permute-done | bytes 16416 | tf_op jit(solution)/shard_map/ppermute | solution.py:40
  341.2 4.6 collective-permute-done.83
  351.0 4.3 collective-permute-done.85
  362.6 4.7 collective-permute-done.86
  374.0 6.2 %collective-permute-done.87 = bf16[128,16,32]{0,2,1:T(8,128)(2,1)} collective-permute-done((bf16[128,16,32]{0,2,1:T(8,128)(2,1)}, bf16[128,16,32]{0,2,1:T(8,128)(2,1)}, u32[]{:S(2)}, u32[]{:S(2)}) %collective-permute-start.87) | collective-permute-done | bytes 131104 | tf_op jit(solution)/shard_map/ppermute | solution.py:28
  395.2 5.4 %collective-permute-start.72 = (f32[16,1,256]{2,1,0:T(1,128)S(1)}, f32[16,1,256]{2,1,0:T(1,128)S(1)}, u32[]{:S(2)}, u32[]{:S(2)}) collective-permute-start(f32[16,1,256]{2,1,0:T(1,128)S(1)} %get-tuple-element.278), channel_id=1, source_target_pairs={{4,0},{8,4},{12,8},{16,12},{20,16},{24,20},{28,24},{32,28},{36,32}... | collective-permute-start | bytes 49160 | tf_op jit(solution)/shard_map/ppermute | solution.py:41
  402.6 7.9 %collective-permute-done.73 = f32[16,1,256]{2,1,0:T(1,128)S(1)} collective-permute-done((f32[16,1,256]{2,1,0:T(1,128)S(1)}, f32[16,1,256]{2,1,0:T(1,128)S(1)}, u32[]{:S(2)}, u32[]{:S(2)}) %collective-permute-start.73) | collective-permute-done | bytes 16416 | tf_op jit(solution)/shard_map/ppermute | solution.py:40
  418.8 5.9 %collective-permute-done.77 = f32[16,1,256]{2,1,0:T(1,128)S(1)} collective-permute-done((f32[16,1,256]{2,1,0:T(1,128)S(1)}, f32[16,1,256]{2,1,0:T(1,128)S(1)}, u32[]{:S(2)}, u32[]{:S(2)}) %collective-permute-start.77) | collective-permute-done | bytes 16416 | tf_op jit(solution)/shard_map/ppermute | solution.py:40
  435.0 4.5 collective-permute-done.89
  448.2 5.9 %collective-permute-done.93 = f32[16,1,256]{2,1,0:T(1,128)S(1)} collective-permute-done((f32[16,1,256]{2,1,0:T(1,128)S(1)}, f32[16,1,256]{2,1,0:T(1,128)S(1)}, u32[]{:S(2)}, u32[]{:S(2)}) %collective-permute-start.93) | collective-permute-done | bytes 16416 | tf_op jit(solution)/shard_map/ppermute | solution.py:40
  462.9 5.9 %collective-permute-done.97 = f32[16,1,256]{2,1,0:T(1,128)S(1)} collective-permute-done((f32[16,1,256]{2,1,0:T(1,128)S(1)}, f32[16,1,256]{2,1,0:T(1,128)S(1)}, u32[]{:S(2)}, u32[]{:S(2)}) %collective-permute-start.97) | collective-permute-done | bytes 16416 | tf_op jit(solution)/shard_map/ppermute | solution.py:40
  477.2 5.9 %collective-permute-done.101 = f32[16,1,256]{2,1,0:T(1,128)S(1)} collective-permute-done((f32[16,1,256]{2,1,0:T(1,128)S(1)}, f32[16,1,256]{2,1,0:T(1,128)S(1)}, u32[]{:S(2)}, u32[]{:S(2)}) %collective-permute-start.101) | collective-permute-done | bytes 16416 | tf_op jit(solution)/shard_map/ppermute | solution.py:40
  (582 shorter events, 282.7 us)
Async XLA Ops:
  0.6 17.2 %collective-permute-start.8 = (f32[1,4,32]{2,1,0:T(4,128)}, f32[1,4,32]{2,1,0:T(4,128)S(1)}, u32[]{:S(2)}, u32[]{:S(2)}) collective-permute-start(f32[1,4,32]{2,1,0:T(4,128)} %bitcast.177), channel_id=1, source_target_pairs={{0,1},{1,0},{2,3},{3,2},{4,5},{5,4},{6,7},{7,6},{8,9},{9,8},{10,11... | collective-permute-start | bytes 1544 | tf_op jit(solution)/shard_map/ppermute | solution.py:28
  1.4 18.3 %collective-permute-start = (bf16[1,16,32]{2,1,0:T(8,128)(2,1)S(1)}, bf16[1,16,32]{2,1,0:T(8,128)(2,1)S(1)}, u32[]{:S(2)}, u32[]{:S(2)}) collective-permute-start(bf16[1,16,32]{2,1,0:T(8,128)(2,1)S(1)} %convert_bitcast_fusion.3), channel_id=1, source_target_pairs={{0,1},{1,0},{2,3},{3,2},{4,5},{5,4},{6,7},{7,6},{8,9},{9,8},{10,11... | collective-permute-start | bytes 3080 | tf_op jit(solution)/shard_map/ppermute | solution.py:28
  3.5 115.0 %collective-permute-start.18 = (f32[16,8,1]{2,1,0:T(8,128)}, f32[16,8,1]{2,1,0:T(8,128)}, u32[]{:S(2)}, u32[]{:S(2)}) collective-permute-start(f32[16,8,1]{2,1,0:T(8,128)} %get-tuple-element.360), channel_id=1, source_target_pairs={{0,3},{1,0},{2,1},{3,2},{4,7},{5,4},{6,5},{7,6},{8,11},{9,8},{10,9... | collective-permute-start | bytes 1544 | tf_op jit(solution)/shard_map/ppermute | solution.py:43
  6.2 112.4 %collective-permute-start.19 = (f32[16,8,1]{2,1,0:T(8,128)}, f32[16,8,1]{2,1,0:T(8,128)}, u32[]{:S(2)}, u32[]{:S(2)}) collective-permute-start(f32[16,8,1]{2,1,0:T(8,128)} %get-tuple-element.359), channel_id=1, source_target_pairs={{0,1},{1,2},{2,3},{3,0},{4,5},{5,6},{6,7},{7,4},{8,9},{9,10},{10,1... | collective-permute-start | bytes 1544 | tf_op jit(solution)/shard_map/ppermute | solution.py:42
  6.8 111.7 %collective-permute-start.16 = (f32[16,1,256]{2,1,0:T(1,128)}, f32[16,1,256]{2,1,0:T(1,128)}, u32[]{:S(2)}, u32[]{:S(2)}) collective-permute-start(f32[16,1,256]{2,1,0:T(1,128)} %get-tuple-element.364), channel_id=1, source_target_pairs={{4,0},{8,4},{12,8},{16,12},{20,16},{24,20},{28,24},{32,28},{36,32}... | collective-permute-start | bytes 49160 | tf_op jit(solution)/shard_map/ppermute | solution.py:41
  17.8 100.8 %collective-permute-start.17 = (f32[16,1,256]{2,1,0:T(1,128)}, f32[16,1,256]{2,1,0:T(1,128)}, u32[]{:S(2)}, u32[]{:S(2)}) collective-permute-start(f32[16,1,256]{2,1,0:T(1,128)} %get-tuple-element.363), channel_id=1, source_target_pairs={{0,4},{4,8},{8,12},{12,16},{16,20},{20,24},{24,28},{28,32},{32,36}... | collective-permute-start | bytes 49160 | tf_op jit(solution)/shard_map/ppermute | solution.py:40
  75.8 12.4 %collective-permute-start.6 = (bf16[64,16,32]{2,1,0:T(8,128)(2,1)S(1)}, bf16[64,16,32]{2,1,0:T(8,128)(2,1)S(1)}, u32[]{:S(2)}, u32[]{:S(2)}) collective-permute-start(bf16[64,16,32]{2,1,0:T(8,128)(2,1)S(1)} %pad_maximum_fusion), channel_id=1, source_target_pairs={{0,64},{1,65},{2,66},{3,67},{4,68},{5,69},{6,70},{7,71},{8,72},{9,... | collective-permute-start | bytes 196616 | tf_op jit(solution)/shard_map/ppermute | solution.py:28
  138.5 12.5 %collective-permute-start.38 = (bf16[64,16,32]{2,1,0:T(8,128)(2,1)S(1)}, bf16[64,16,32]{2,1,0:T(8,128)(2,1)S(1)}, u32[]{:S(2)}, u32[]{:S(2)}) collective-permute-start(bf16[64,16,32]{2,1,0:T(8,128)(2,1)S(1)} %pad_maximum_fusion.1), channel_id=1, source_target_pairs={{0,64},{1,65},{2,66},{3,67},{4,68},{5,69},{6,70},{7,71},{8,72},{9,... | collective-permute-start | bytes 196616 | tf_op jit(solution)/shard_map/ppermute | solution.py:28
  139.2 24.2 %collective-permute-start.22 = (f32[16,8,1]{2,1,0:T(8,128)}, f32[16,8,1]{2,1,0:T(8,128)}, u32[]{:S(2)}, u32[]{:S(2)}) collective-permute-start(f32[16,8,1]{2,1,0:T(8,128)} %get-tuple-element.352), channel_id=1, source_target_pairs={{0,3},{1,0},{2,1},{3,2},{4,7},{5,4},{6,5},{7,6},{8,11},{9,8},{10,9... | collective-permute-start | bytes 1544 | tf_op jit(solution)/shard_map/ppermute | solution.py:43
  139.2 24.2 %collective-permute-start.23 = (f32[16,8,1]{2,1,0:T(8,128)S(1)}, f32[16,8,1]{2,1,0:T(8,128)}, u32[]{:S(2)}, u32[]{:S(2)}) collective-permute-start(f32[16,8,1]{2,1,0:T(8,128)S(1)} %get-tuple-element.351), channel_id=1, source_target_pairs={{0,1},{1,2},{2,3},{3,0},{4,5},{5,6},{6,7},{7,4},{8,9},{9,10},{10,1... | collective-permute-start | bytes 1544 | tf_op jit(solution)/shard_map/ppermute | solution.py:42
  139.7 23.6 %collective-permute-start.20 = (f32[16,1,256]{2,1,0:T(1,128)}, f32[16,1,256]{2,1,0:T(1,128)}, u32[]{:S(2)}, u32[]{:S(2)}) collective-permute-start(f32[16,1,256]{2,1,0:T(1,128)} %get-tuple-element.356), channel_id=1, source_target_pairs={{4,0},{8,4},{12,8},{16,12},{20,16},{24,20},{28,24},{32,28},{36,32}... | collective-permute-start | bytes 49160 | tf_op jit(solution)/shard_map/ppermute | solution.py:41
  149.0 14.3 %collective-permute-start.21 = (f32[16,1,256]{2,1,0:T(1,128)}, f32[16,1,256]{2,1,0:T(1,128)}, u32[]{:S(2)}, u32[]{:S(2)}) collective-permute-start(f32[16,1,256]{2,1,0:T(1,128)} %get-tuple-element.355), channel_id=1, source_target_pairs={{0,4},{4,8},{8,12},{12,16},{16,20},{20,24},{24,28},{28,32},{32,36}... | collective-permute-start | bytes 49160 | tf_op jit(solution)/shard_map/ppermute | solution.py:40
  151.8 18.8 %collective-permute-start.39 = (bf16[128,16,32]{0,2,1:T(8,128)(2,1)S(1)}, bf16[128,16,32]{0,2,1:T(8,128)(2,1)}, u32[]{:S(2)}, u32[]{:S(2)}) collective-permute-start(bf16[128,16,32]{0,2,1:T(8,128)(2,1)S(1)} %pad_maximum_fusion.8), channel_id=1, source_target_pairs={{0,128},{1,129},{2,130},{3,131},{4,132},{5,133},{6,134},{7,135},{8... | collective-permute-start | bytes 393224 | tf_op jit(solution)/shard_map/ppermute | solution.py:28
  184.2 13.7 %collective-permute-start.26 = (f32[16,8,1]{2,1,0:T(8,128)S(1)}, f32[16,8,1]{2,1,0:T(8,128)S(1)}, u32[]{:S(2)}, u32[]{:S(2)}) collective-permute-start(f32[16,8,1]{2,1,0:T(8,128)S(1)} %get-tuple-element.344), channel_id=1, source_target_pairs={{0,3},{1,0},{2,1},{3,2},{4,7},{5,4},{6,5},{7,6},{8,11},{9,8},{10,9... | collective-permute-start | bytes 1544 | tf_op jit(solution)/shard_map/ppermute | solution.py:43
  186.6 11.2 %collective-permute-start.27 = (f32[16,8,1]{2,1,0:T(8,128)S(1)}, f32[16,8,1]{2,1,0:T(8,128)S(1)}, u32[]{:S(2)}, u32[]{:S(2)}) collective-permute-start(f32[16,8,1]{2,1,0:T(8,128)S(1)} %get-tuple-element.343), channel_id=1, source_target_pairs={{0,1},{1,2},{2,3},{3,0},{4,5},{5,6},{6,7},{7,4},{8,9},{9,10},{10,1... | collective-permute-start | bytes 1544 | tf_op jit(solution)/shard_map/ppermute | solution.py:42
  186.6 11.2 %collective-permute-start.24 = (f32[16,1,256]{2,1,0:T(1,128)S(1)}, f32[16,1,256]{2,1,0:T(1,128)S(1)}, u32[]{:S(2)}, u32[]{:S(2)}) collective-permute-start(f32[16,1,256]{2,1,0:T(1,128)S(1)} %get-tuple-element.348), channel_id=1, source_target_pairs={{4,0},{8,4},{12,8},{16,12},{20,16},{24,20},{28,24},{32,28},{36,32}... | collective-permute-start | bytes 49160 | tf_op jit(solution)/shard_map/ppermute | solution.py:41
  210.1 9.9 %collective-permute-start.29 = (f32[16,1,256]{2,1,0:T(1,128)S(1)}, f32[16,1,256]{2,1,0:T(1,128)S(1)}, u32[]{:S(2)}, u32[]{:S(2)}) collective-permute-start(f32[16,1,256]{2,1,0:T(1,128)S(1)} %get-tuple-element.339), channel_id=1, source_target_pairs={{0,4},{4,8},{8,12},{12,16},{16,20},{20,24},{24,28},{28,32},{32,36}... | collective-permute-start | bytes 49160 | tf_op jit(solution)/shard_map/ppermute | solution.py:40
  235.9 9.9 %collective-permute-start.41 = (f32[16,1,256]{2,1,0:T(1,128)S(1)}, f32[16,1,256]{2,1,0:T(1,128)S(1)}, u32[]{:S(2)}, u32[]{:S(2)}) collective-permute-start(f32[16,1,256]{2,1,0:T(1,128)S(1)} %get-tuple-element.329), channel_id=1, source_target_pairs={{0,4},{4,8},{8,12},{12,16},{16,20},{20,24},{24,28},{28,32},{32,36}... | collective-permute-start | bytes 49160 | tf_op jit(solution)/shard_map/ppermute | solution.py:40
  239.9 14.1 %collective-permute-start.60 = (bf16[16,16,32]{2,1,0:T(8,128)(2,1)S(1)}, bf16[16,16,32]{2,1,0:T(8,128)(2,1)S(1)}, u32[]{:S(2)}, u32[]{:S(2)}) collective-permute-start(bf16[16,16,32]{2,1,0:T(8,128)(2,1)S(1)} %pad_maximum_fusion.17), channel_id=1, source_target_pairs={{0,16},{1,17},{2,18},{3,19},{4,20},{5,21},{6,22},{7,23},{8,24},{9,... | collective-permute-start | bytes 49160 | tf_op jit(solution)/shard_map/ppermute | solution.py:28
  250.1 9.9 %collective-permute-start.45 = (f32[16,1,256]{2,1,0:T(1,128)S(1)}, f32[16,1,256]{2,1,0:T(1,128)S(1)}, u32[]{:S(2)}, u32[]{:S(2)}) collective-permute-start(f32[16,1,256]{2,1,0:T(1,128)S(1)} %get-tuple-element.321), channel_id=1, source_target_pairs={{0,4},{4,8},{8,12},{12,16},{16,20},{20,24},{24,28},{28,32},{32,36}... | collective-permute-start | bytes 49160 | tf_op jit(solution)/shard_map/ppermute | solution.py:40
  254.1 28.7 %collective-permute-start.61 = (bf16[32,16,32]{2,1,0:T(8,128)(2,1)S(1)}, bf16[32,16,32]{2,1,0:T(8,128)(2,1)S(1)}, u32[]{:S(2)}, u32[]{:S(2)}) collective-permute-start(bf16[32,16,32]{2,1,0:T(8,128)(2,1)S(1)} %pad_maximum_fusion.9), channel_id=1, source_target_pairs={{0,32},{1,33},{2,34},{3,35},{4,36},{5,37},{6,38},{7,39},{8,40},{9,... | collective-permute-start | bytes 98312 | tf_op jit(solution)/shard_map/ppermute | solution.py:28
  264.6 9.9 %collective-permute-start.49 = (f32[16,1,256]{2,1,0:T(1,128)S(1)}, f32[16,1,256]{2,1,0:T(1,128)S(1)}, u32[]{:S(2)}, u32[]{:S(2)}) collective-permute-start(f32[16,1,256]{2,1,0:T(1,128)S(1)} %get-tuple-element.311), channel_id=1, source_target_pairs={{0,4},{4,8},{8,12},{12,16},{16,20},{20,24},{24,28},{28,32},{32,36}... | collective-permute-start | bytes 49160 | tf_op jit(solution)/shard_map/ppermute | solution.py:40
  278.9 9.9 %collective-permute-start.53 = (f32[16,1,256]{2,1,0:T(1,128)S(1)}, f32[16,1,256]{2,1,0:T(1,128)S(1)}, u32[]{:S(2)}, u32[]{:S(2)}) collective-permute-start(f32[16,1,256]{2,1,0:T(1,128)S(1)} %get-tuple-element.303), channel_id=1, source_target_pairs={{0,4},{4,8},{8,12},{12,16},{16,20},{20,24},{24,28},{28,32},{32,36}... | collective-permute-start | bytes 49160 | tf_op jit(solution)/shard_map/ppermute | solution.py:40
  283.7 15.0 %collective-permute-start.62 = (bf16[64,16,32]{2,1,0:T(8,128)(2,1)}, bf16[64,16,32]{2,1,0:T(8,128)(2,1)}, u32[]{:S(2)}, u32[]{:S(2)}) collective-permute-start(bf16[64,16,32]{2,1,0:T(8,128)(2,1)} %pad_maximum_fusion.2), channel_id=1, source_target_pairs={{0,64},{1,65},{2,66},{3,67},{4,68},{5,69},{6,70},{7,71},{8,72},{9,... | collective-permute-start | bytes 196616 | tf_op jit(solution)/shard_map/ppermute | solution.py:28
  300.4 10.0 %collective-permute-start.63 = (bf16[128,16,32]{0,2,1:T(8,128)(2,1)S(1)}, bf16[128,16,32]{0,2,1:T(8,128)(2,1)S(1)}, u32[]{:S(2)}, u32[]{:S(2)}) collective-permute-start(bf16[128,16,32]{0,2,1:T(8,128)(2,1)S(1)} %pad_maximum_fusion.10), channel_id=1, source_target_pairs={{0,128},{1,129},{2,130},{3,131},{4,132},{5,133},{6,134},{7,135},{8... | collective-permute-start | bytes 393224 | tf_op jit(solution)/shard_map/ppermute | solution.py:28
  321.5 10.8 %collective-permute-start.81 = (bf16[2,16,32]{2,1,0:T(8,128)(2,1)S(1)}, bf16[2,16,32]{2,1,0:T(8,128)(2,1)S(1)}, u32[]{:S(2)}, u32[]{:S(2)}) collective-permute-start(bf16[2,16,32]{2,1,0:T(8,128)(2,1)S(1)} %pad_maximum_fusion.33), channel_id=1, source_target_pairs={{0,2},{1,3},{2,0},{3,1},{4,6},{5,7},{6,4},{7,5},{8,10},{9,11},{10,... | collective-permute-start | bytes 6152 | tf_op jit(solution)/shard_map/ppermute | solution.py:28
  355.5 11.8 %collective-permute-start.86 = (bf16[64,16,32]{2,1,0:T(8,128)(2,1)S(1)}, bf16[64,16,32]{2,1,0:T(8,128)(2,1)S(1)}, u32[]{:S(2)}, u32[]{:S(2)}) collective-permute-start(bf16[64,16,32]{2,1,0:T(8,128)(2,1)S(1)} %pad_maximum_fusion.3), channel_id=1, source_target_pairs={{0,64},{1,65},{2,66},{3,67},{4,68},{5,69},{6,70},{7,71},{8,72},{9,... | collective-permute-start | bytes 196616 | tf_op jit(solution)/shard_map/ppermute | solution.py:28
  356.2 13.1 %collective-permute-start.70 = (f32[16,8,1]{2,1,0:T(8,128)}, f32[16,8,1]{2,1,0:T(8,128)}, u32[]{:S(2)}, u32[]{:S(2)}) collective-permute-start(f32[16,8,1]{2,1,0:T(8,128)} %get-tuple-element.282), channel_id=1, source_target_pairs={{0,3},{1,0},{2,1},{3,2},{4,7},{5,4},{6,5},{7,6},{8,11},{9,8},{10,9... | collective-permute-start | bytes 1544 | tf_op jit(solution)/shard_map/ppermute | solution.py:43
  356.2 13.1 %collective-permute-start.71 = (f32[16,8,1]{2,1,0:T(8,128)S(1)}, f32[16,8,1]{2,1,0:T(8,128)}, u32[]{:S(2)}, u32[]{:S(2)}) collective-permute-start(f32[16,8,1]{2,1,0:T(8,128)S(1)} %get-tuple-element.281), channel_id=1, source_target_pairs={{0,1},{1,2},{2,3},{3,0},{4,5},{5,6},{6,7},{7,4},{8,9},{9,10},{10,1... | collective-permute-start | bytes 1544 | tf_op jit(solution)/shard_map/ppermute | solution.py:42
  356.7 12.6 %collective-permute-start.68 = (f32[16,1,256]{2,1,0:T(1,128)}, f32[16,1,256]{2,1,0:T(1,128)}, u32[]{:S(2)}, u32[]{:S(2)}) collective-permute-start(f32[16,1,256]{2,1,0:T(1,128)} %get-tuple-element.286), channel_id=1, source_target_pairs={{4,0},{8,4},{12,8},{16,12},{20,16},{24,20},{28,24},{32,28},{36,32}... | collective-permute-start | bytes 49160 | tf_op jit(solution)/shard_map/ppermute | solution.py:41
  360.6 10.2 %collective-permute-start.69 = (f32[16,1,256]{2,1,0:T(1,128)}, f32[16,1,256]{2,1,0:T(1,128)}, u32[]{:S(2)}, u32[]{:S(2)}) collective-permute-start(f32[16,1,256]{2,1,0:T(1,128)} %get-tuple-element.285), channel_id=1, source_target_pairs={{0,4},{4,8},{8,12},{12,16},{16,20},{20,24},{24,28},{28,32},{32,36}... | collective-permute-start | bytes 49160 | tf_op jit(solution)/shard_map/ppermute | solution.py:40
  368.7 11.5 %collective-permute-start.87 = (bf16[128,16,32]{0,2,1:T(8,128)(2,1)}, bf16[128,16,32]{0,2,1:T(8,128)(2,1)}, u32[]{:S(2)}, u32[]{:S(2)}) collective-permute-start(bf16[128,16,32]{0,2,1:T(8,128)(2,1)} %pad_maximum_fusion.12), channel_id=1, source_target_pairs={{0,128},{1,129},{2,130},{3,131},{4,132},{5,133},{6,134},{7,135},{8... | collective-permute-start | bytes 393224 | tf_op jit(solution)/shard_map/ppermute | solution.py:28
  (115 other events, 698.8 us)
